TPU v7x, 256 devices: a whole 4x4x8 slice. The times are simulated.
256 devices in a mesh: row: 16 (over z_hi, x, core), col: 16 (over y, z_lo).
Axes of the slice: x: 4, y: 4, z: 8 (z_hi: 2, z_lo: 4; z = z_hi * 4 + z_lo), core: 2. Of those that a mesh axis runs over, the one named last changes fastest.
Arguments:
- points: float32 [64, 32768], P(None, ('row', 'col')), may hold values from -24 to 24, as said below
- embedding: float32 [2, 32768], P(None, ('row', 'col')), may hold values from -8 to 8
- precision: float32 [32768], P(('row', 'col')), may hold values from 0.05 to 2
Outputs:
- force: float32 [2, 32768], P(None, ('row', 'col'))
- calibrated: float32 [32768], P(('row', 'col'))
Inputs may be any that keep to these rules, and one draw needn't show every extreme that they name: `points`: each point's coordinates are normal values times a positive scale of that point.
All inputs are finite; a program needn't handle non-finite values.
Results may differ from a plain program's by a relative error of at most 0.0003.
Values sent between devices are 32-bit elements; how exact they have to be, the bound alone decides.
No kernel may reach another device: no remote copies, remote signals or barrier semaphores. Data moves between devices by JAX's collectives and lax.ppermute only.
A program may use at most 64 MiB of HBM per device.

v0:
```python
import math
import jax
import jax.numpy as jnp
from jax import lax
from jax.sharding import PartitionSpec as P

PERP = 30


def newton_update(zsum, first, second, start_prec):
    entropy = jnp.log(zsum) + start_prec * first / zsum
    spread = second / zsum - (first / zsum) ** 2
    factor = jnp.clip(
        (entropy - math.log(PERP)) / jnp.maximum(start_prec * start_prec * spread, 1.0), -2.0, 2.0
    )
    return start_prec * jnp.exp(factor)


def col_stage(values):
    count = lax.axis_size("col")
    held = values
    shift = 1
    while shift < count:
        pairs = [(i, (i + shift) % count) for i in range(count)]
        held = jnp.concatenate([held, lax.ppermute(held, "col", pairs)], axis=1)
        shift *= 2
    return held


def spread_all(values):
    return lax.all_gather(col_stage(values), "row", axis=1, tiled=True)


def body(points, embedding, precision):
    per_dev = points.shape[1]
    width = points.shape[0]
    axes = ("row", "col")
    own_start = lax.axis_index("row") * lax.axis_size("col") * per_dev
    own_coords = points
    own_map = embedding
    own_sq = jnp.sum(own_coords * own_coords, axis=0)
    packed = jnp.concatenate([points, embedding, own_sq[None, :]], axis=0)
    every = spread_all(packed)
    total = every.shape[1]
    all_coords = every[:width]
    all_map = every[width : width + 2]
    all_sq = every[width + 2]
    inner = lax.dot_general(
        own_coords,
        all_coords,
        (((0,), (0,)), ((), ())),
        precision=lax.Precision.HIGHEST,
        preferred_element_type=jnp.float32,
    )
    distance = jnp.maximum(own_sq[:, None] + all_sq[None, :] - 2.0 * inner, 0.0)
    col_ids = jnp.arange(total, dtype=jnp.int32)[None, :]
    row_ids = (own_start + jnp.arange(per_dev, dtype=jnp.int32))[:, None]
    itself = row_ids == col_ids
    nearest = jnp.min(jnp.where(itself, jnp.inf, distance), axis=1)
    shifted = distance - nearest[:, None]
    expo = jnp.where(itself, 0.0, jnp.exp(-precision[:, None] * shifted))
    zsum = jnp.sum(expo, axis=1)
    first = jnp.sum(expo * shifted, axis=1)
    second = jnp.sum(expo * shifted * shifted, axis=1)
    calib = newton_update(zsum, first, second, precision)
    norm = jnp.sum(jnp.where(itself, 0.0, jnp.exp(-calib[:, None] * shifted)), axis=1)
    delta_a = own_map[0][:, None] - all_map[0][None, :]
    delta_b = own_map[1][:, None] - all_map[1][None, :]
    kernel = jnp.where(itself, 0.0, 1.0 / (1.0 + delta_a * delta_a + delta_b * delta_b))
    kernel_part = jnp.sum(kernel)
    qslot = jnp.where(jnp.arange(per_dev) == 0, kernel_part, 0.0)
    stats = jnp.stack([calib, nearest, 1.0 / norm, qslot])
    all_stats = spread_all(stats)
    calib_cols = all_stats[0]
    nearest_cols = all_stats[1]
    inv_norm_cols = all_stats[2]
    qsum = jnp.sum(all_stats[3])
    cond_rows = jnp.exp(-calib[:, None] * shifted) * (1.0 / norm)[:, None]
    cond_cols = (
        jnp.exp(-calib_cols[None, :] * (distance - nearest_cols[None, :])) * inv_norm_cols[None, :]
    )
    affinity = jnp.where(itself, 0.0, 0.5 * (cond_rows + cond_cols))
    coef = (affinity - total * kernel / qsum) * kernel
    force = jnp.stack([jnp.sum(coef * delta_a, axis=1), jnp.sum(coef * delta_b, axis=1)])
    return (force, calib)


def solution(mesh):
    in_specs = (P(None, ("row", "col")), P(None, ("row", "col")), P(("row", "col")))
    out_specs = (P(None, ("row", "col")), P(("row", "col")))
    return jax.shard_map(body, mesh=mesh, in_specs=in_specs, out_specs=out_specs, check_vma=False)
```

profile of v0, /device:TPU:1, one launch (start us, length us, event | category | flops | bytes accessed | tf_op | source)
XLA Modules:
  0.0 310.4 jit_solution(2971438880049326950)
XLA Ops:
  7.2 0.0 all-gather.2.cloned.1.call-start
  7.2 0.8 multiply_reduce_fusion.1
  8.0 0.8 pad_maximum_fusion.3
  8.8 2.5 collective-permute-start
  11.2 6.5 %collective-permute-done = f32[67,128]{1,0:T(8,128)S(1)} collective-permute-done((f32[67,128]{1,0:T(8,128)S(1)}, f32[67,128]{1,0:T(8,128)S(1)}, u32[]{:S(2)}, u32[]{:S(2)}) %collective-permute-start) | collective-permute-done | bytes 34336 | tf_op jit(solution)/shard_map/ppermute | solution.py:25
  17.7 0.8 pad_maximum_fusion.2
  18.5 0.0 collective-permute-start.1
  18.6 6.2 %collective-permute-done.1 = f32[67,256]{1,0:T(8,128)S(1)} collective-permute-done((f32[67,256]{1,0:T(8,128)S(1)}, f32[67,256]{1,0:T(8,128)S(1)}, u32[]{:S(2)}, u32[]{:S(2)}) %collective-permute-start.1) | collective-permute-done | bytes 68640 | tf_op jit(solution)/shard_map/ppermute | solution.py:25
  24.8 0.8 pad_maximum_fusion.1
  25.5 0.1 collective-permute-start.2
  25.6 5.2 %collective-permute-done.2 = f32[67,512]{1,0:T(8,128)S(1)} collective-permute-done((f32[67,512]{1,0:T(8,128)S(1)}, f32[67,512]{1,0:T(8,128)S(1)}, u32[]{:S(2)}, u32[]{:S(2)}) %collective-permute-start.2) | collective-permute-done | bytes 137248 | tf_op jit(solution)/shard_map/ppermute | solution.py:25
  30.8 0.8 pad_maximum_fusion
  31.6 0.1 collective-permute-start.3
  31.8 7.0 %collective-permute-done.3 = f32[67,1024]{1,0:T(8,128)S(1)} collective-permute-done((f32[67,1024]{1,0:T(8,128)S(1)}, f32[67,1024]{1,0:T(8,128)S(1)}, u32[]{:S(2)}, u32[]{:S(2)}) %collective-permute-start.3) | collective-permute-done | bytes 274464 | tf_op jit(solution)/shard_map/ppermute | solution.py:25
  38.8 0.0 copy-start
  38.8 0.8 copy-done
  39.6 0.0 all-gather.2.cloned.1.call-update
  39.6 0.7 neg.12
  40.3 0.8 slice_bitcast_fusion.1
  41.1 118.7 %all-gather.2.cloned.1.call-done = f32[67,32768]{1,0:T(8,128)} async-done(((f32[67,2048]{1,0:T(8,128)}), f32[67,32768]{1,0:T(8,128)}) %all-gather.2.cloned.1.call-update) | async-done | bytes 8781840 | tf_op jit(solution)/shard_map/all_gather | solution.py:31
  159.8 2.6 fusion.15
  162.4 40.7 %select_reduce_fusion.1 = (f32[128]{0:T(128)S(1)}, f32[128,32768]{0,1:T(8,128)S(1)}) fusion(s32[128]{0:T(128)S(1)} %iota_add_fusion, f32[64,128]{1,0:T(8,128)} %param.3, f32[67,32768]{1,0:T(8,128)} %all-gather.2.cloned.1.call-done, f32[32768]{0:T(1024)S(1)} %bitcast.31, f32[128]{0:T(128)S(1)} %multiply_reduce_fusion.1), kind=kOutput, calls=%fused_computation.22 | convolution fusion | flops 3250585600 | bytes 25331200 | tf_op jit(solution)/shard_map/dot_general | solution.py:48
  203.2 0.0 copy-start.2
  203.2 6.6 %multiply_reduce_fusion = (f32[128]{0:T(128)S(1)}, f32[128]{0:T(128)S(1)}, f32[128]{0:T(128)S(1)}) fusion(f32[128,32768]{0,1:T(8,128)S(1)} %get-tuple-element.25, f32[128]{0:T(128)S(1)} %get-tuple-element.24, f32[128]{0:T(128)S(1)} %neg.12, s32[128]{0:T(128)S(1)} %iota_add_fusion), kind=kLoop, calls=%fused_computation.17 | loop fusion | flops 37748352 | bytes 16780288 | tf_op jit(solution)/shard_map/reduce_sum | solution.py:64
  209.7 0.0 copy-done.2
  209.8 0.0 copy-start.1
  209.8 17.8 %select_reduce_fusion = (f32[128]{0:T(128)S(1)}, f32[]{:T(128)}) fusion(f32[128,32768]{0,1:T(8,128)S(1)} %get-tuple-element.25, f32[128]{0:T(128)S(1)} %get-tuple-element.9, f32[128]{0:T(128)S(1)} %get-tuple-element.24, s32[128]{0:T(128)S(1)} %iota_add_fusion, f32[32768]{0:T(1024)S(1)} %bitcast.26, f32[128]{0:T(128)S(1)} %get-tuple-element.23, ...), kind=kLoop, calls=%fused_computation.15 | loop fusion | flops 58720128 | bytes 17042436 | tf_op jit(solution)/shard_map/reduce_sum | solution.py:66
  227.5 0.6 compare_select_fusion
  228.2 0.3 collective-permute-start.4
  228.5 6.1 %collective-permute-done.4 = f32[4,128]{1,0:T(4,128)S(1)} collective-permute-done((f32[4,128]{1,0:T(4,128)S(1)}, f32[4,128]{1,0:T(4,128)S(1)}, u32[]{:S(2)}, u32[]{:S(2)}) %collective-permute-start.4) | collective-permute-done | bytes 2080 | tf_op jit(solution)/shard_map/ppermute | solution.py:25
  234.7 0.1 collective-permute-start.5
  234.8 5.4 %collective-permute-done.5 = f32[4,256]{1,0:T(4,128)S(1)} collective-permute-done((f32[4,256]{1,0:T(4,128)S(1)}, f32[4,256]{1,0:T(4,128)S(1)}, u32[]{:S(2)}, u32[]{:S(2)}) %collective-permute-start.5) | collective-permute-done | bytes 4128 | tf_op jit(solution)/shard_map/ppermute | solution.py:25
  240.2 0.1 collective-permute-start.6
  240.3 3.7 %collective-permute-done.6 = f32[4,512]{1,0:T(4,128)S(1)} collective-permute-done((f32[4,512]{1,0:T(4,128)S(1)}, f32[4,512]{1,0:T(4,128)S(1)}, u32[]{:S(2)}, u32[]{:S(2)}) %collective-permute-start.6) | collective-permute-done | bytes 8224 | tf_op jit(solution)/shard_map/ppermute | solution.py:25
  244.0 0.1 collective-permute-start.7
  244.1 4.1 %collective-permute-done.7 = f32[4,1024]{1,0:T(4,128)S(1)} collective-permute-done((f32[4,1024]{1,0:T(4,128)S(1)}, f32[4,1024]{1,0:T(4,128)S(1)}, u32[]{:S(2)}, u32[]{:S(2)}) %collective-permute-start.7) | collective-permute-done | bytes 16416 | tf_op jit(solution)/shard_map/ppermute | solution.py:25
  248.2 30.1 %all_gather.7 = f32[4,32768]{1,0:T(4,128)S(1)} all-gather(f32[4,2048]{1,0:T(4,128)S(1)} %constant_dynamic-update-slice_fusion.5), channel_id=1, replica_groups=mesh['row'=16,'col'=16] {'row'}, dimensions={1}, use_global_device_ids=true | all-gather | bytes 557056 | tf_op jit(solution)/shard_map/all_gather | solution.py:31
  278.3 1.0 slice_negate_fusion
  279.3 23.7 %fusion.7 = (f32[128]{0:T(128)S(1)}, f32[128]{0:T(128)S(1)}) fusion(f32[32768]{0:T(1024)S(1)} %bitcast.25, f32[128]{0:T(128)S(1)} %get-tuple-element.22, f32[32768]{0:T(1024)S(1)} %bitcast.27, f32[128]{0:T(128)S(1)} %get-tuple-element.23, f32[]{:T(128)} %get-tuple-element.15, f32[32768]{0:T(1024)S(1)} %bitcast.29, f32[128,32768]{0,1:T(8,128)S(1)} %get-tuple-element.25, ...), kind=kLoop, calls=%fused_computation.12 | loop fusion | flops 109051648 | bytes 17436676 | tf_op jit(solution)/shard_map/reduce_sum | solution.py:84
  303.0 0.0 copy-done.1
  303.0 0.6 pad_maximum_fusion.8
  (16 shorter events, 0.2 us)
Async XLA Ops:
  7.2 152.6 %all-gather.2.cloned.1.call-start = ((), (), s32[]{:S(2)}) async-start(), calls=%async_computation | async-start | bytes 10027008 | tf_op jit(solution)/shard_map/all_gather | solution.py:31
  8.8 9.0 %collective-permute-start = (f32[67,128]{1,0:T(8,128)S(1)}, f32[67,128]{1,0:T(8,128)S(1)}, u32[]{:S(2)}, u32[]{:S(2)}) collective-permute-start(f32[67,128]{1,0:T(8,128)S(1)} %get-tuple-element.18), channel_id=1, source_target_pairs={{0,1},{1,2},{2,3},{3,4},{4,5},{5,6},{6,7},{7,8},{8,9},{9,10},{10,1... | collective-permute-start | bytes 102920 | tf_op jit(solution)/shard_map/ppermute | solution.py:25
  18.5 6.2 %collective-permute-start.1 = (f32[67,256]{1,0:T(8,128)S(1)}, f32[67,256]{1,0:T(8,128)S(1)}, u32[]{:S(2)}, u32[]{:S(2)}) collective-permute-start(f32[67,256]{1,0:T(8,128)S(1)} %pad_maximum_fusion.2), channel_id=1, source_target_pairs={{0,2},{1,3},{2,4},{3,5},{4,6},{5,7},{6,8},{7,9},{8,10},{9,11},{10,... | collective-permute-start | bytes 205832 | tf_op jit(solution)/shard_map/ppermute | solution.py:25
  25.5 5.3 %collective-permute-start.2 = (f32[67,512]{1,0:T(8,128)S(1)}, f32[67,512]{1,0:T(8,128)S(1)}, u32[]{:S(2)}, u32[]{:S(2)}) collective-permute-start(f32[67,512]{1,0:T(8,128)S(1)} %pad_maximum_fusion.1), channel_id=1, source_target_pairs={{0,4},{1,5},{2,6},{3,7},{4,8},{5,9},{6,10},{7,11},{8,12},{9,13},{1... | collective-permute-start | bytes 411656 | tf_op jit(solution)/shard_map/ppermute | solution.py:25
  31.6 7.2 %collective-permute-start.3 = (f32[67,1024]{1,0:T(8,128)S(1)}, f32[67,1024]{1,0:T(8,128)S(1)}, u32[]{:S(2)}, u32[]{:S(2)}) collective-permute-start(f32[67,1024]{1,0:T(8,128)S(1)} %pad_maximum_fusion), channel_id=1, source_target_pairs={{0,8},{1,9},{2,10},{3,11},{4,12},{5,13},{6,14},{7,15},{8,0},{9,1},... | collective-permute-start | bytes 823304 | tf_op jit(solution)/shard_map/ppermute | solution.py:25
  38.8 0.8 copy-start
  203.2 6.6 %copy-start.2 = (f32[128]{0:T(128)S(1)}, f32[128]{0:T(128)}, u32[]{:S(2)}) copy-start(f32[128]{0:T(128)} %param.5) | copy-start | bytes 1540
  209.8 93.2 %copy-start.1 = (f32[128]{0:T(128)}, f32[128]{0:T(128)S(1)}, u32[]{:S(2)}) copy-start(f32[128]{0:T(128)S(1)} %get-tuple-element.10) | copy-start | bytes 1540
  228.2 6.4 %collective-permute-start.4 = (f32[4,128]{1,0:T(4,128)S(1)}, f32[4,128]{1,0:T(4,128)S(1)}, u32[]{:S(2)}, u32[]{:S(2)}) collective-permute-start(f32[4,128]{1,0:T(4,128)S(1)} %get-tuple-element.20), channel_id=1, source_target_pairs={{0,1},{1,2},{2,3},{3,4},{4,5},{5,6},{6,7},{7,8},{8,9},{9,10},{10,1... | collective-permute-start | bytes 6152 | tf_op jit(solution)/shard_map/ppermute | solution.py:25
  234.7 5.5 %collective-permute-start.5 = (f32[4,256]{1,0:T(4,128)S(1)}, f32[4,256]{1,0:T(4,128)S(1)}, u32[]{:S(2)}, u32[]{:S(2)}) collective-permute-start(f32[4,256]{1,0:T(4,128)S(1)} %pad_maximum_fusion.6), channel_id=1, source_target_pairs={{0,2},{1,3},{2,4},{3,5},{4,6},{5,7},{6,8},{7,9},{8,10},{9,11},{10,... | collective-permute-start | bytes 12296 | tf_op jit(solution)/shard_map/ppermute | solution.py:25
  240.2 3.8 %collective-permute-start.6 = (f32[4,512]{1,0:T(4,128)S(1)}, f32[4,512]{1,0:T(4,128)S(1)}, u32[]{:S(2)}, u32[]{:S(2)}) collective-permute-start(f32[4,512]{1,0:T(4,128)S(1)} %pad_maximum_fusion.5), channel_id=1, source_target_pairs={{0,4},{1,5},{2,6},{3,7},{4,8},{5,9},{6,10},{7,11},{8,12},{9,13},{1... | collective-permute-start | bytes 24584 | tf_op jit(solution)/shard_map/ppermute | solution.py:25
  244.0 4.2 %collective-permute-start.7 = (f32[4,1024]{1,0:T(4,128)S(1)}, f32[4,1024]{1,0:T(4,128)S(1)}, u32[]{:S(2)}, u32[]{:S(2)}) collective-permute-start(f32[4,1024]{1,0:T(4,128)S(1)} %pad_maximum_fusion.4), channel_id=1, source_target_pairs={{0,8},{1,9},{2,10},{3,11},{4,12},{5,13},{6,14},{7,15},{8,0},{9,1},... | collective-permute-start | bytes 49160 | tf_op jit(solution)/shard_map/ppermute | solution.py:25
Sparse Core Ops, SparseCore 0:
  39.8 119.9 all-gather.1
where the time goes:
time: 311 us; the launch traced here: 310 us
  waiting for transfers between devices  163 us (52%)
  other arithmetic  54.9 us (18%)
  matrix products  40.7 us (13%)
  blocking collectives  30.1 us (10%)
  between operations  14.2 us (5%)
  local copies, waits for them, and re-layouts  4.27 us (1%)
  starting transfers between devices  3.27 us (1%)
    all_gather x1, waiting for transfers between devices, spread_all(): return lax.all_gather(col_stage(values), 'row', axis=1, tiled=True)  119 us
    ppermute x8, waiting for transfers between devices, col_stage(): held = jnp.concatenate([held, lax.ppermute(held, 'col', pairs)], axis=1)  44.2 us
    dot_general x1, matrix products, body(): lax.dot_general(own_coords, all_coords, (((0,), (0,)), ((), ())), precisi...  40.7 us
    all_gather x1, blocking collectives, spread_all(): return lax.all_gather(col_stage(values), 'row', axis=1, tiled=True)  30.1 us
    reduce_sum x1, other arithmetic, body(): jnp.sum(coef * delta_a, axis=1)  23.7 us
    reduce_sum x1, other arithmetic, body(): jnp.sum(jnp.where(itself, 0.0, jnp.exp(-calib[:, None] * shifted)), axis=1)  17.8 us
    reduce_sum x1, other arithmetic, body(): second = jnp.sum(expo * shifted * shifted, axis=1)  6.56 us
  transfers between devices with their start and end apart: 9, of which 9 were waited for; matrix products, arithmetic and copies ran while one was open for 0% of the time, Pallas kernels for 0%

commit v1 on v0

--- a/solution.py
+++ b/solution.py
@@ -3,6 +3,7 @@
 import jax.numpy as jnp
 from jax import lax
 from jax.sharding import PartitionSpec as P
+from jax.lax import all_to_all, psum
 
 PERP = 30
 
@@ -28,7 +29,9 @@
 
 
 def spread_all(values):
-    return lax.all_gather(col_stage(values), "row", axis=1, tiled=True)
+    return jnp.concatenate(
+        all_to_all(jnp.stack(psum(1, "row") * [col_stage(values)]), "row", 0, 0), axis=1
+    )
 
 
 def body(points, embedding, precision):

time: 311 us -> 456 us (1.47)
  waiting for transfers between devices: 163 us -> 293 us
  starting transfers between devices: 3.27 us -> 49.3 us
  blocking collectives: 30.1 us -> 0 us
  between operations: 14.2 us -> 0.87 us
  local copies, waits for them, and re-layouts: 4.27 us -> 13.4 us
    all_to_all x0 -> x2, waiting for transfers between devices: none -> 253 us  [spread_all(): all_to_all(jnp.stack(psum(1, 'row') * [col_stage(values)]), 'row', 0, 0)]
    all_gather x1 -> x0, waiting for transfers between devices: 119 us -> none  [spread_all(): return lax.all_gather(col_stage(values), 'row', axis=1, tiled=True)]
    all_to_all x0 -> x2, starting transfers between devices: none -> 33.5 us  [spread_all(): all_to_all(jnp.stack(psum(1, 'row') * [col_stage(values)]), 'row', 0, 0)]
    all_gather x1 -> x0, blocking collectives: 30.1 us -> none  [spread_all(): return lax.all_gather(col_stage(values), 'row', axis=1, tiled=True)]
    ppermute x8, starting transfers between devices: 3.23 us -> 15.8 us  [col_stage(): held = jnp.concatenate([held, lax.ppermute(held, 'col', pairs)], axis=1)]
    another operation x0 -> x2, local copies, waits for them, and re-layouts: none -> 5.73 us  [spread_all(): jnp.stack(psum(1, 'row') * [col_stage(values)])]
    ppermute x8, waiting for transfers between devices: 44.2 us -> 39.5 us  [col_stage(): held = jnp.concatenate([held, lax.ppermute(held, 'col', pairs)], axis=1)]
  transfers between devices with their start and end apart: 9 -> 10, of which waited for: 9 -> 10; matrix products, arithmetic and copies ran while one was open for 0% -> 0% of each run, Pallas kernels for 0% -> 0%
where the time goes in v1:
time: 456 us; the launch traced here: 452 us
  waiting for transfers between devices  293 us (64%)
  other arithmetic  56.9 us (12%)
  starting transfers between devices  49.3 us (11%)
  matrix products  39.2 us (9%)
  local copies, waits for them, and re-layouts  13.4 us (3%)
    all_to_all x2, waiting for transfers between devices, spread_all(): all_to_all(jnp.stack(psum(1, 'row') * [col_stage(values)]), 'row', 0, 0)  253 us
    ppermute x8, waiting for transfers between devices, col_stage(): held = jnp.concatenate([held, lax.ppermute(held, 'col', pairs)], axis=1)  39.5 us
    dot_general x1, matrix products, body(): lax.dot_general(own_coords, all_coords, (((0,), (0,)), ((), ())), precisi...  39.2 us
    all_to_all x2, starting transfers between devices, spread_all(): all_to_all(jnp.stack(psum(1, 'row') * [col_stage(values)]), 'row', 0, 0)  33.5 us
    reduce_sum x1, other arithmetic, body(): jnp.sum(coef * delta_a, axis=1)  26.3 us
    reduce_sum x1, other arithmetic, body(): jnp.sum(jnp.where(itself, 0.0, jnp.exp(-calib[:, None] * shifted)), axis=1)  17.8 us
    ppermute x8, starting transfers between devices, col_stage(): held = jnp.concatenate([held, lax.ppermute(held, 'col', pairs)], axis=1)  15.8 us
  transfers between devices with their start and end apart: 10, of which 10 were waited for; matrix products, arithmetic and copies ran while one was open for 0% of the time, Pallas kernels for 0%

profile of v1, /device:TPU:1, one launch (start us, length us, event | category | flops | bytes accessed | tf_op | source)
XLA Modules:
  0.0 452.5 jit_solution(18343177491798030475)
XLA Ops:
  0.6 0.0 copy-start.2
  0.6 0.0 copy-start.4
  0.7 0.8 multiply_reduce_fusion.1
  1.4 0.8 pad_maximum_fusion.3
  2.2 2.5 collective-permute-start
  4.7 6.5 %collective-permute-done = f32[67,128]{1,0:T(8,128)S(1)} collective-permute-done((f32[67,128]{1,0:T(8,128)S(1)}, f32[67,128]{1,0:T(8,128)S(1)}, u32[]{:S(2)}, u32[]{:S(2)}) %collective-permute-start) | collective-permute-done | bytes 34336 | tf_op jit(solution)/shard_map/ppermute | solution.py:26
  11.2 0.8 pad_maximum_fusion.2
  12.0 0.0 collective-permute-start.1
  12.0 6.2 %collective-permute-done.1 = f32[67,256]{1,0:T(8,128)S(1)} collective-permute-done((f32[67,256]{1,0:T(8,128)S(1)}, f32[67,256]{1,0:T(8,128)S(1)}, u32[]{:S(2)}, u32[]{:S(2)}) %collective-permute-start.1) | collective-permute-done | bytes 68640 | tf_op jit(solution)/shard_map/ppermute | solution.py:26
  18.2 0.8 pad_maximum_fusion.1
  19.0 0.1 collective-permute-start.2
  19.1 5.2 %collective-permute-done.2 = f32[67,512]{1,0:T(8,128)S(1)} collective-permute-done((f32[67,512]{1,0:T(8,128)S(1)}, f32[67,512]{1,0:T(8,128)S(1)}, u32[]{:S(2)}, u32[]{:S(2)}) %collective-permute-start.2) | collective-permute-done | bytes 137248 | tf_op jit(solution)/shard_map/ppermute | solution.py:26
  24.3 0.8 pad_maximum_fusion
  25.1 0.1 collective-permute-start.3
  25.2 7.0 %collective-permute-done.3 = f32[67,1024]{1,0:T(8,128)S(1)} collective-permute-done((f32[67,1024]{1,0:T(8,128)S(1)}, f32[67,1024]{1,0:T(8,128)S(1)}, u32[]{:S(2)}, u32[]{:S(2)}) %collective-permute-start.3) | collective-permute-done | bytes 274464 | tf_op jit(solution)/shard_map/ppermute | solution.py:26
  32.3 4.8 %stack.16 = f32[16,67,2048]{2,1,0:T(8,128)} broadcast(f32[67,2048]{1,0:T(8,128)S(1)} %constant_dynamic-update-slice_fusion), dimensions={1,2} | broadcast | bytes 9330688 | tf_op jit(solution)/shard_map/stack | solution.py:33
  37.1 14.8 %all-to-all-start = ((f32[16,67,2048]{2,1,0:T(8,128)}), f32[16,67,2048]{2,1,0:T(8,128)}, u32[]{:S(2)}, u32[]{:S(2)}) async-start(f32[16,67,2048]{2,1,0:T(8,128)} %stack.16), calls=%async_computation | async-start | bytes 18874368 | tf_op jit(solution)/shard_map/all_to_all | solution.py:33
  51.9 0.0 copy-done.4
  51.9 0.0 copy-done.2
  51.9 238.7 %all-to-all-done = f32[16,67,2048]{2,1,0:T(8,128)} async-done(((f32[16,67,2048]{2,1,0:T(8,128)}), f32[16,67,2048]{2,1,0:T(8,128)}, u32[]{:S(2)}, u32[]{:S(2)}) %all-to-all-start) | async-done | bytes 8781856 | tf_op jit(solution)/shard_map/all_to_all | solution.py:33
  290.7 2.5 fusion.14
  293.1 0.0 copy-start.1
  293.1 4.0 slice_bitcast_fusion
  297.1 1.1 copy.10
  298.2 0.0 copy-done.1
  298.2 39.2 %select_reduce_fusion.1 = (f32[128]{0:T(128)S(1)}, f32[128,32768]{0,1:T(8,128)S(1)}) fusion(s32[128]{0:T(128)S(1)} %iota_add_fusion, f32[64,32768]{1,0:T(8,128)S(1)} %bitcast.30, f32[64,128]{1,0:T(8,128)S(1)} %copy-done.1, f32[32768]{0:T(1024)S(1)} %bitcast.39, f32[128]{0:T(128)S(1)} %multiply_reduce_fusion.1), kind=kOutput, calls=%fused_computation.22 | convolution fusion | flops 3250585600 | bytes 25331200 | tf_op jit(solution)/shard_map/dot_general | solution.py:51
  337.5 0.0 copy-start
  337.5 6.6 %multiply_reduce_fusion = (f32[128]{0:T(128)S(1)}, f32[128]{0:T(128)S(1)}, f32[128]{0:T(128)S(1)}) fusion(f32[128,32768]{0,1:T(8,128)S(1)} %get-tuple-element.25, f32[128]{0:T(128)S(1)} %get-tuple-element.24, f32[128]{0:T(128)S(1)} %neg.20, s32[128]{0:T(128)S(1)} %iota_add_fusion), kind=kLoop, calls=%fused_computation.17 | loop fusion | flops 37748352 | bytes 16780288 | tf_op jit(solution)/shard_map/reduce_sum | solution.py:67
  344.1 0.0 copy-start.3
  344.1 17.8 %select_reduce_fusion = (f32[128]{0:T(128)S(1)}, f32[]{:T(128)}) fusion(f32[128,32768]{0,1:T(8,128)S(1)} %get-tuple-element.25, f32[128]{0:T(128)S(1)} %get-tuple-element.9, f32[128]{0:T(128)S(1)} %get-tuple-element.24, s32[128]{0:T(128)S(1)} %iota_add_fusion, f32[32768]{0:T(1024)S(1)} %bitcast.34, f32[128]{0:T(128)S(1)} %get-tuple-element.23, ...), kind=kLoop, calls=%fused_computation.15 | loop fusion | flops 58720128 | bytes 17042436 | tf_op jit(solution)/shard_map/reduce_sum | solution.py:69
  361.9 0.0 copy-done
  361.9 0.6 compare_select_fusion
  362.6 0.1 collective-permute-start.4
  362.6 6.3 %collective-permute-done.4 = f32[4,128]{1,0:T(4,128)S(1)} collective-permute-done((f32[4,128]{1,0:T(4,128)S(1)}, f32[4,128]{1,0:T(4,128)S(1)}, u32[]{:S(2)}, u32[]{:S(2)}) %collective-permute-start.4) | collective-permute-done | bytes 2080 | tf_op jit(solution)/shard_map/ppermute | solution.py:26
  369.0 0.1 collective-permute-start.5
  369.1 5.4 %collective-permute-done.5 = f32[4,256]{1,0:T(4,128)S(1)} collective-permute-done((f32[4,256]{1,0:T(4,128)S(1)}, f32[4,256]{1,0:T(4,128)S(1)}, u32[]{:S(2)}, u32[]{:S(2)}) %collective-permute-start.5) | collective-permute-done | bytes 4128 | tf_op jit(solution)/shard_map/ppermute | solution.py:26
  374.5 10.8 %collective-permute-start.6 = (f32[4,512]{1,0:T(4,128)S(1)}, f32[4,512]{1,0:T(4,128)S(1)}, u32[]{:S(2)}, u32[]{:S(2)}) collective-permute-start(f32[4,512]{1,0:T(4,128)S(1)} %pad_maximum_fusion.5), channel_id=1, source_target_pairs={{0,4},{1,5},{2,6},{3,7},{4,8},{5,9},{6,10},{7,11},{8,12},{9,13},{1... | collective-permute-start | bytes 24584 | tf_op jit(solution)/shard_map/ppermute | solution.py:26
  385.4 0.8 collective-permute-done.6
  386.2 2.1 collective-permute-start.7
  388.3 2.0 collective-permute-done.7
  390.4 0.9 stack.20
  391.2 18.7 %all-to-all-start.1 = ((f32[16,4,2048]{2,1,0:T(4,128)}), f32[16,4,2048]{2,1,0:T(4,128)S(1)}, u32[]{:S(2)}, u32[]{:S(2)}) async-start(f32[16,4,2048]{2,1,0:T(4,128)} %stack.20), calls=%async_computation.1 | async-start | bytes 1048576 | tf_op jit(solution)/shard_map/all_to_all | solution.py:33
  410.0 14.6 %all-to-all-done.1 = f32[16,4,2048]{2,1,0:T(4,128)S(1)} async-done(((f32[16,4,2048]{2,1,0:T(4,128)}), f32[16,4,2048]{2,1,0:T(4,128)S(1)}, u32[]{:S(2)}, u32[]{:S(2)}) %all-to-all-start.1) | async-done | bytes 524320 | tf_op jit(solution)/shard_map/all_to_all | solution.py:33
  424.6 1.0 slice_negate_fusion
  425.6 26.3 %fusion.7 = (f32[128]{0:T(128)S(1)}, f32[128]{0:T(128)S(1)}) fusion(f32[32768]{0:T(1024)S(1)} %bitcast.33, f32[128]{0:T(128)S(1)} %get-tuple-element.22, f32[32768]{0:T(1024)S(1)} %bitcast.35, f32[128]{0:T(128)S(1)} %get-tuple-element.23, f32[]{:T(128)} %get-tuple-element.15, f32[32768]{0:T(1024)S(1)} %bitcast.37, f32[128,32768]{0,1:T(8,128)} %copy-done, ...), kind=kLoop, calls=%fused_computation.12 | loop fusion | flops 109051648 | bytes 17436676 | tf_op jit(solution)/shard_map/reduce_sum | solution.py:87
  451.9 0.0 copy-done.3
  451.9 0.6 pad_maximum_fusion.8
  (18 shorter events, 0.2 us)
Async XLA Ops:
  0.6 51.3 %copy-start.2 = (f32[2,128]{1,0:T(2,128)S(1)}, f32[2,128]{1,0:T(2,128)}, u32[]{:S(2)}) copy-start(f32[2,128]{1,0:T(2,128)} %param.4) | copy-start | bytes 3076
  0.6 51.3 %copy-start.4 = (f32[128]{0:T(128)S(1)}, f32[128]{0:T(128)}, u32[]{:S(2)}) copy-start(f32[128]{0:T(128)} %param.5) | copy-start | bytes 1540
  2.2 9.0 %collective-permute-start = (f32[67,128]{1,0:T(8,128)S(1)}, f32[67,128]{1,0:T(8,128)S(1)}, u32[]{:S(2)}, u32[]{:S(2)}) collective-permute-start(f32[67,128]{1,0:T(8,128)S(1)} %get-tuple-element.18), channel_id=1, source_target_pairs={{0,1},{1,2},{2,3},{3,4},{4,5},{5,6},{6,7},{7,8},{8,9},{9,10},{10,1... | collective-permute-start | bytes 102920 | tf_op jit(solution)/shard_map/ppermute | solution.py:26
  12.0 6.2 %collective-permute-start.1 = (f32[67,256]{1,0:T(8,128)S(1)}, f32[67,256]{1,0:T(8,128)S(1)}, u32[]{:S(2)}, u32[]{:S(2)}) collective-permute-start(f32[67,256]{1,0:T(8,128)S(1)} %pad_maximum_fusion.2), channel_id=1, source_target_pairs={{0,2},{1,3},{2,4},{3,5},{4,6},{5,7},{6,8},{7,9},{8,10},{9,11},{10,... | collective-permute-start | bytes 205832 | tf_op jit(solution)/shard_map/ppermute | solution.py:26
  19.0 5.3 %collective-permute-start.2 = (f32[67,512]{1,0:T(8,128)S(1)}, f32[67,512]{1,0:T(8,128)S(1)}, u32[]{:S(2)}, u32[]{:S(2)}) collective-permute-start(f32[67,512]{1,0:T(8,128)S(1)} %pad_maximum_fusion.1), channel_id=1, source_target_pairs={{0,4},{1,5},{2,6},{3,7},{4,8},{5,9},{6,10},{7,11},{8,12},{9,13},{1... | collective-permute-start | bytes 411656 | tf_op jit(solution)/shard_map/ppermute | solution.py:26
  25.1 7.2 %collective-permute-start.3 = (f32[67,1024]{1,0:T(8,128)S(1)}, f32[67,1024]{1,0:T(8,128)S(1)}, u32[]{:S(2)}, u32[]{:S(2)}) collective-permute-start(f32[67,1024]{1,0:T(8,128)S(1)} %pad_maximum_fusion), channel_id=1, source_target_pairs={{0,8},{1,9},{2,10},{3,11},{4,12},{5,13},{6,14},{7,15},{8,0},{9,1},... | collective-permute-start | bytes 823304 | tf_op jit(solution)/shard_map/ppermute | solution.py:26
  37.1 253.6 %all-to-all-start = ((f32[16,67,2048]{2,1,0:T(8,128)}), f32[16,67,2048]{2,1,0:T(8,128)}, u32[]{:S(2)}, u32[]{:S(2)}) async-start(f32[16,67,2048]{2,1,0:T(8,128)} %stack.16), calls=%async_computation | async-start | bytes 18874368 | tf_op jit(solution)/shard_map/all_to_all | solution.py:33
  293.1 5.1 %copy-start.1 = (f32[64,128]{1,0:T(8,128)S(1)}, f32[64,128]{1,0:T(8,128)}, u32[]{:S(2)}) copy-start(f32[64,128]{1,0:T(8,128)} %param.3) | copy-start | bytes 98308
  337.5 24.4 %copy-start = (f32[128,32768]{0,1:T(8,128)}, f32[128,32768]{0,1:T(8,128)S(1)}, u32[]{:S(2)}) copy-start(f32[128,32768]{0,1:T(8,128)S(1)} %get-tuple-element.25) | copy-start | bytes 50331652
  344.1 107.8 %copy-start.3 = (f32[128]{0:T(128)}, f32[128]{0:T(128)S(1)}, u32[]{:S(2)}) copy-start(f32[128]{0:T(128)S(1)} %get-tuple-element.10) | copy-start | bytes 1540
  362.6 6.4 %collective-permute-start.4 = (f32[4,128]{1,0:T(4,128)S(1)}, f32[4,128]{1,0:T(4,128)S(1)}, u32[]{:S(2)}, u32[]{:S(2)}) collective-permute-start(f32[4,128]{1,0:T(4,128)S(1)} %get-tuple-element.20), channel_id=1, source_target_pairs={{0,1},{1,2},{2,3},{3,4},{4,5},{5,6},{6,7},{7,8},{8,9},{9,10},{10,1... | collective-permute-start | bytes 6152 | tf_op jit(solution)/shard_map/ppermute | solution.py:26
  369.0 5.5 %collective-permute-start.5 = (f32[4,256]{1,0:T(4,128)S(1)}, f32[4,256]{1,0:T(4,128)S(1)}, u32[]{:S(2)}, u32[]{:S(2)}) collective-permute-start(f32[4,256]{1,0:T(4,128)S(1)} %pad_maximum_fusion.6), channel_id=1, source_target_pairs={{0,2},{1,3},{2,4},{3,5},{4,6},{5,7},{6,8},{7,9},{8,10},{9,11},{10,... | collective-permute-start | bytes 12296 | tf_op jit(solution)/shard_map/ppermute | solution.py:26
  374.5 11.6 %collective-permute-start.6 = (f32[4,512]{1,0:T(4,128)S(1)}, f32[4,512]{1,0:T(4,128)S(1)}, u32[]{:S(2)}, u32[]{:S(2)}) collective-permute-start(f32[4,512]{1,0:T(4,128)S(1)} %pad_maximum_fusion.5), channel_id=1, source_target_pairs={{0,4},{1,5},{2,6},{3,7},{4,8},{5,9},{6,10},{7,11},{8,12},{9,13},{1... | collective-permute-start | bytes 24584 | tf_op jit(solution)/shard_map/ppermute | solution.py:26
  386.2 4.2 collective-permute-start.7
  391.2 33.3 %all-to-all-start.1 = ((f32[16,4,2048]{2,1,0:T(4,128)}), f32[16,4,2048]{2,1,0:T(4,128)S(1)}, u32[]{:S(2)}, u32[]{:S(2)}) async-start(f32[16,4,2048]{2,1,0:T(4,128)} %stack.20), calls=%async_computation.1 | async-start | bytes 1048576 | tf_op jit(solution)/shard_map/all_to_all | solution.py:33
